TPU v7x, 512 devices: a whole 4x4x16 slice. The times are simulated.
512 devices in a mesh: dp: 64 (over y, z), tensor: 8 (over x, core).
Axes of the slice: x: 4, y: 4, z: 16, core: 2. Of those that a mesh axis runs over, the one named last changes fastest.
Arguments:
- tokens: bfloat16 [65536, 1408], P(('dp', 'tensor')), may hold values from -6 to 6
- ln1_gain: float32 [1408], replicated, may hold values from 0.1 to 1.9
- ln1_shift: float32 [1408], replicated, may hold values from -3 to 3
- w_qkv: bfloat16 [1408, 16, 264], P(None, 'tensor')
- w_out: bfloat16 [16, 88, 1408], P('tensor'), may hold values from -0.625 to 0.625
- ln2_gain: float32 [1408], replicated, may hold values from 0.1 to 1.9
- ln2_shift: float32 [1408], replicated, may hold values from -3 to 3
- w_proj: bfloat16 [5632, 3584], P('dp', 'tensor'), may hold values from -0.078125 to 0.078125
- proj_bias: float32 [3584], P('tensor'), may hold values from -3 to 3
- segments: int32 [64, 256], P('dp'), may hold values from 0 to 7, never falling along the last dimension, each value on 1 to 128 neighbouring positions
- owners: int32 [16384, 1], P('dp'), may hold values from 0 to 63; in each aligned block of 256 rows (0 to 255, 256 to 511, ...) at most 8 rows name the same one
Outputs:
- delivered: bfloat16 [32768, 3584], P('dp', 'tensor')
Inputs may be any that keep to these rules, and one draw needn't show every extreme that they name: `segments`: within a pack numbers never fall, every image has 1 to 128 groups and one has exactly that many. `owners`: among the 256 merged tokens of one pack no owner gets more than 8; in some pack an owner gets exactly 8.
All inputs are finite; a program needn't handle non-finite values.
Results may differ from a plain program's by a relative error of at most 0.015.
Values may be sent and summed in bfloat16 or wider, within the bound.
No kernel may reach another device: no remote copies, remote signals or barrier semaphores. Data moves between devices by JAX's collectives and lax.ppermute only.
A program may use at most 64 MiB of HBM per device.

v0:
```python
import jax
import jax.numpy as jnp
from jax import lax
from jax.sharding import PartitionSpec as P


def layer_norm(values, gain, shift):
    wide = values.astype(jnp.float32)
    average = jnp.mean(wide, axis=-1, keepdims=True)
    centred = wide - average
    variance = jnp.mean(centred * centred, axis=-1, keepdims=True)
    return centred * lax.rsqrt(variance + 1e-06) * gain + shift


def attend(heads_qkv, token_segs):
    row_count = heads_qkv.shape[0]
    width = heads_qkv.shape[2] // 3
    queries = heads_qkv[:, :, :width]
    keys_all = heads_qkv[:, :, width : 2 * width]
    values_all = heads_qkv[:, :, 2 * width :]
    score_scale = 1.0 / jnp.sqrt(jnp.float32(width))
    block_rows = min(512, row_count)
    outputs = []
    for block_index in range(row_count // block_rows):
        lower = block_index * block_rows
        scores = (
            jnp.einsum(
                "qhd,khd->hqk",
                queries[lower : lower + block_rows],
                keys_all,
                preferred_element_type=jnp.float32,
            )
            * score_scale
        )
        same = token_segs[lower : lower + block_rows][:, None] == token_segs[None, :]
        scores = jnp.where(same[None], scores, -jnp.inf)
        row_max = jnp.max(scores, axis=-1, keepdims=True)
        exponent = jnp.exp(scores - row_max)
        probs = (exponent / jnp.sum(exponent, axis=-1, keepdims=True)).astype(jnp.bfloat16)
        context = jnp.einsum("hqk,khd->qhd", probs, values_all, preferred_element_type=jnp.float32)
        outputs.append(context.astype(jnp.bfloat16))
    return jnp.concatenate(outputs, axis=0)


def shards(
    tokens,
    ln1_gain,
    ln1_shift,
    w_qkv,
    w_out,
    ln2_gain,
    ln2_shift,
    w_proj,
    proj_bias,
    segments,
    owners,
):
    dp_count = lax.axis_size("dp")
    tp_count = lax.axis_size("tensor")
    w_proj_all = lax.all_gather(w_proj, "dp", axis=0, tiled=True)
    w_out_all = lax.all_gather(w_out, "tensor", axis=0, tiled=True)
    gathered = lax.all_gather(tokens, "tensor", axis=0, tiled=True)
    row_count = gathered.shape[0]
    local_rows = tokens.shape[0]
    normed = layer_norm(gathered, ln1_gain, ln1_shift).astype(jnp.bfloat16)
    heads_here = w_qkv.shape[1]
    heads_qkv = jnp.dot(
        normed, w_qkv.reshape(w_qkv.shape[0], -1), preferred_element_type=jnp.float32
    )
    heads_qkv = heads_qkv.astype(jnp.bfloat16).reshape(row_count, heads_here, -1)
    token_segs = jnp.repeat(segments[0], 4)
    context = attend(heads_qkv, token_segs).reshape(tp_count, local_rows, -1)
    context_mine = lax.all_to_all(context, "tensor", split_axis=0, concat_axis=0, tiled=True)
    out_heads = w_out_all.reshape(tp_count, -1, w_out_all.shape[2])
    attn = jnp.einsum("sqd,sdo->qo", context_mine, out_heads, preferred_element_type=jnp.float32)
    hidden = (tokens.astype(jnp.float32) + attn).astype(jnp.bfloat16)
    normed_two = layer_norm(hidden, ln2_gain, ln2_shift).astype(jnp.bfloat16)
    merged_mine = normed_two.reshape(local_rows // 4, -1)
    merged = lax.all_gather(merged_mine, "tensor", axis=0, tiled=True)
    groups = merged.shape[0]
    summed = jnp.dot(merged, w_proj_all, preferred_element_type=jnp.float32)
    projected = (summed + proj_bias).astype(jnp.bfloat16)
    dests = owners[:, 0]
    onehot = (dests[:, None] == jnp.arange(dp_count, dtype=jnp.int32)[None, :]).astype(jnp.int32)
    earlier = jnp.cumsum(onehot, axis=0) - onehot
    position = jnp.sum(earlier * onehot, axis=1)
    capacity = 2 * groups // dp_count
    slot_index = dests * capacity + position
    scatter_table = (
        slot_index[None, :] == jnp.arange(dp_count * capacity, dtype=jnp.int32)[:, None]
    ).astype(jnp.bfloat16)
    outgoing = jnp.dot(scatter_table, projected, preferred_element_type=jnp.float32).astype(
        jnp.bfloat16
    )
    outgoing = outgoing.reshape(dp_count, capacity, -1)
    arrived = lax.all_to_all(outgoing, "dp", split_axis=0, concat_axis=0, tiled=True)
    return arrived.reshape(dp_count * capacity, -1)


def solution(mesh):
    return jax.shard_map(
        shards,
        mesh=mesh,
        in_specs=(
            P(("dp", "tensor"), None),
            P(),
            P(),
            P(None, "tensor", None),
            P("tensor", None, None),
            P(),
            P(),
            P("dp", "tensor"),
            P("tensor"),
            P("dp", None),
            P("dp", None),
        ),
        out_specs=P("dp", "tensor"),
        check_vma=False,
    )
```

profile of v0, /device:TPU:8, one launch (start us, length us, event | category | flops | bytes accessed | tf_op | source)
XLA Modules:
  0.0 339.7 jit_solution(10978495204272725188)
XLA Ops:
  6.5 0.0 copy-start
  6.5 0.0 copy-start.7
  6.5 0.0 copy-start.6
  6.5 0.0 all-gather.5.cloned.1.call-start
  6.5 0.7 all-gather.5.cloned.1.call-update
  7.3 0.0 all-gather.7.cloned.1.call-start
  7.3 0.7 all-gather.7.cloned.1.call-update
  8.0 0.0 all-gather.11.cloned.1.call-start
  8.1 0.7 all-gather.11.cloned.1.call-update
  8.7 0.0 all-gather.9.cloned.1.call-start
  8.8 0.7 slice_bitcast_fusion.1
  9.5 0.1 broadcast_in_dim.24
  9.5 0.1 eq.84
  9.7 0.1 broadcast_in_dim.28
  9.7 0.1 eq.89
  9.9 0.8 broadcast_in_dim.25
  10.6 0.1 eq.86
  10.8 0.7 broadcast_compare_fusion.1
  11.4 36.8 %all-gather.5.cloned.1.call-done = bf16[1024,1408]{1,0:T(8,128)(2,1)} async-done(((bf16[128,1408]{1,0:T(8,128)(2,1)}), bf16[1024,1408]{1,0:T(8,128)(2,1)}) %all-gather.5.cloned.1.call-update) | async-done | bytes 2883600 | tf_op jit(solution)/shard_map/all_gather | solution.py:62
  48.2 0.0 copy-start.1
  48.2 2.4 convert_reduce_fusion
  50.6 0.3 copy-done.1
  50.9 0.9 fusion.4
  51.8 0.0 copy-done
  51.8 0.0 copy-done.7
  51.8 0.0 copy-done.6
  51.8 3.1 fusion.27
  55.0 4.8 %fusion.82 = (f32[2,512]{1,0:T(2,128)S(1)}, f32[2,512,1024]{2,1,0:T(8,128)}) fusion(pred[512,1024]{1,0:T(8,128)(4,1)S(1)} %get-tuple-element.5, bf16[1024,2,264]{0,2,1:T(8,128)(2,1)} %bitcast.63), kind=kOutput, calls=%fused_computation.86 | convolution fusion | flops 188744704 | bytes 5263360 | tf_op jit(solution)/shard_map/sub | solution.py:38
  59.8 0.0 copy-start.9
  59.8 4.8 %fusion.73 = (f32[2,512]{1,0:T(2,128)S(1)}, f32[2,512,1024]{2,1,0:T(8,128)}) fusion(pred[512,1024]{1,0:T(8,128)(4,1)S(1)} %get-tuple-element.6, bf16[1024,2,264]{0,2,1:T(8,128)(2,1)} %bitcast.64), kind=kOutput, calls=%fused_computation.85 | convolution fusion | flops 188744704 | bytes 5263360 | tf_op jit(solution)/shard_map/sub | solution.py:38
  64.6 0.0 copy-done.9
  64.6 0.0 copy-start.10
  64.6 3.2 fusion.33
  67.8 0.4 copy-done.10
  68.2 0.0 copy-start.2
  68.2 0.9 fusion.34
  69.1 0.0 copy-start.4
  69.1 0.0 copy-start.5
  69.1 0.1 copy.22
  69.3 16.0 %all_to_all.10 = bf16[8,128,176]{1,2,0:T(8,128)(2,1)S(1)} all-to-all(bf16[8,128,176]{1,2,0:T(8,128)(2,1)S(1)} %copy.18), channel_id=1, replica_groups=mesh['dp'=64,'tensor'=8] {'tensor'}, dimensions={0} | all-to-all | bytes 720896 | tf_op jit(solution)/shard_map/all_to_all | solution.py:73
  85.2 0.0 copy-start.3
  85.2 8.4 %all-gather.7.cloned.1.call-done = bf16[16,88,1408]{2,1,0:T(8,128)(2,1)} async-done(((bf16[2,88,1408]{2,1,0:T(8,128)(2,1)}), bf16[16,88,1408]{2,1,0:T(8,128)(2,1)}) %all-gather.7.cloned.1.call-update) | async-done | bytes 3964944 | tf_op jit(solution)/shard_map/all_gather | solution.py:61
  93.6 0.0 copy-done.2
  93.7 0.0 copy-start.8
  93.7 3.0 fusion.91
  96.7 0.2 multiply_reduce_fusion
  96.9 0.0 copy-done.4
  96.9 0.0 copy-done.5
  96.9 0.2 add_convert_fusion
  97.1 1.0 reshape.155
  98.1 0.0 all-gather.9.cloned.1.call-update
  98.1 0.0 copy-done.3
  98.2 0.6 reduce-window.6
  98.8 0.2 slice_reduce_fusion
  99.0 0.1 fusion.67
  99.1 146.7 %all-gather.11.cloned.1.call-done = bf16[5632,448]{1,0:T(8,128)(2,1)} async-done(((bf16[88,448]{1,0:T(8,128)(2,1)}), bf16[5632,448]{1,0:T(8,128)(2,1)}) %all-gather.11.cloned.1.call-update) | async-done | bytes 5046288 | tf_op jit(solution)/shard_map/all_gather | solution.py:60
  245.8 32.5 %all-gather.9.cloned.1.call-done = bf16[256,5632]{1,0:T(8,128)(2,1)} async-done(((bf16[32,5632]{1,0:T(8,128)(2,1)}), bf16[256,5632]{1,0:T(8,128)(2,1)}) %all-gather.9.cloned.1.call-update) | async-done | bytes 2883600 | tf_op jit(solution)/shard_map/all_gather | solution.py:79
  278.3 0.0 copy-done.8
  278.3 6.0 %convolution_convert_fusion = bf16[512,448]{0,1:T(8,128)(2,1)S(1)} fusion(bf16[256,5632]{1,0:T(8,128)(2,1)} %all-gather.9.cloned.1.call-done, bf16[5632,448]{1,0:T(8,128)(2,1)} %all-gather.11.cloned.1.call-done, s32[256]{0:T(256)S(1)} %multiply_add_fusion, f32[448]{0:T(512)S(1)} %copy-done.8), kind=kOutput, calls=%fused_computation.36 | convolution fusion | flops 1409875968 | bytes 8391424 | tf_op jit(solution)/shard_map/dot_general | solution.py:92
  284.3 0.2 copy.19
  284.5 47.7 %all_to_all.11 = bf16[64,8,448]{2,1,0:T(8,128)(2,1)S(1)} all-to-all(bf16[64,8,448]{2,1,0:T(8,128)(2,1)S(1)} %bitcast.55), channel_id=1, replica_groups=mesh['dp'=64,'tensor'=8] {'dp'}, dimensions={0} | all-to-all | bytes 917504 | tf_op jit(solution)/shard_map/all_to_all | solution.py:96
  332.2 1.0 copy.20
  (10 shorter events, 0.2 us)
Async XLA Ops:
  6.5 45.3 %copy-start = (bf16[1408,2,264]{0,2,1:T(8,128)(2,1)S(1)}, bf16[1408,2,264]{0,2,1:T(8,128)(2,1)}, u32[]{:S(2)}) copy-start(bf16[1408,2,264]{0,2,1:T(8,128)(2,1)} %param.14) | copy-start | bytes 4460548
  6.5 45.3 %copy-start.7 = (f32[1408]{0:T(1024)S(1)}, f32[1408]{0:T(1024)}, u32[]{:S(2)}) copy-start(f32[1408]{0:T(1024)} %param.12) | copy-start | bytes 16900
  6.5 45.3 %copy-start.6 = (f32[1408]{0:T(1024)S(1)}, f32[1408]{0:T(1024)}, u32[]{:S(2)}) copy-start(f32[1408]{0:T(1024)} %param.13) | copy-start | bytes 16900
  6.5 41.7 %all-gather.5.cloned.1.call-start = ((), (), s32[]{:S(2)}) async-start(), calls=%async_computation.2 | async-start | bytes 3244032 | tf_op jit(solution)/shard_map/all_gather | solution.py:62
  7.3 86.4 %all-gather.7.cloned.1.call-start = ((), (), s32[]{:S(2)}) async-start(), calls=%async_computation.3 | async-start | bytes 4460544 | tf_op jit(solution)/shard_map/all_gather | solution.py:61
  8.0 237.8 %all-gather.11.cloned.1.call-start = ((), (), s32[]{:S(2)}) async-start(), calls=%async_computation.5 | async-start | bytes 5857280 | tf_op jit(solution)/shard_map/all_gather | solution.py:60
  8.7 269.5 %all-gather.9.cloned.1.call-start = ((), (), s32[]{:S(2)}) async-start(), calls=%async_computation.4 | async-start | bytes 3244032 | tf_op jit(solution)/shard_map/all_gather | solution.py:79
  48.2 2.7 copy-start.1
  59.8 4.8 %copy-start.9 = (bf16[1024,528]{0,1:T(8,128)(2,1)S(1)}, bf16[1024,528]{0,1:T(8,128)(2,1)}, u32[]{:S(2)}) copy-start(bf16[1024,528]{0,1:T(8,128)(2,1)} %fusion.27) | copy-start | bytes 3244036
  64.6 3.6 %copy-start.10 = (f32[2,512,1024]{2,1,0:T(8,128)S(1)}, f32[2,512,1024]{2,1,0:T(8,128)}, u32[]{:S(2)}) copy-start(f32[2,512,1024]{2,1,0:T(8,128)} %get-tuple-element.10) | copy-start | bytes 12582916
  68.2 25.5 %copy-start.2 = (bf16[128,1408]{1,0:T(8,128)(2,1)S(1)}, bf16[128,1408]{1,0:T(8,128)(2,1)}, u32[]{:S(2)}) copy-start(bf16[128,1408]{1,0:T(8,128)(2,1)} %param.11) | copy-start | bytes 1081348
  69.1 27.8 %copy-start.4 = (f32[1408]{0:T(1024)S(1)}, f32[1408]{0:T(1024)}, u32[]{:S(2)}) copy-start(f32[1408]{0:T(1024)} %param.17) | copy-start | bytes 16900
  69.1 27.8 %copy-start.5 = (f32[1408]{0:T(1024)S(1)}, f32[1408]{0:T(1024)}, u32[]{:S(2)}) copy-start(f32[1408]{0:T(1024)} %param.16) | copy-start | bytes 16900
  85.2 12.9 %copy-start.3 = (s32[256,1]{0,1:T(1,128)S(1)}, s32[256,1]{0,1:T(1,128)}, u32[]{:S(2)}) copy-start(s32[256,1]{0,1:T(1,128)} %param.21) | copy-start | bytes 3076
  93.7 184.6 %copy-start.8 = (f32[448]{0:T(512)S(1)}, f32[448]{0:T(512)}, u32[]{:S(2)}) copy-start(f32[448]{0:T(512)} %param.19) | copy-start | bytes 5380
Sparse Core Ops, SparseCore 0:
  9.5 38.6 all-gather.4
  50.3 43.2 all-gather.6
  96.6 149.1 all-gather.10
  247.8 30.4 all-gather.8
where the time goes:
time: 340 us
  waiting for transfers between devices  226 us (66%)
  blocking collectives  63.7 us (19%)
  matrix products  25.8 us (8%)
  between operations  13.3 us (4%)
  other arithmetic  5.21 us (2%)
  local copies, waits for them, and re-layouts  5.09 us (1%)
    all_gather x1, waiting for transfers between devices, shards(): w_proj_all = lax.all_gather(w_proj, 'dp', axis=0, tiled=True)  147 us
    all_to_all x1, blocking collectives, shards(): lax.all_to_all(outgoing, 'dp', split_axis=0, concat_axis=0, tiled=True)  47.7 us
    all_gather x1, waiting for transfers between devices, shards(): gathered = lax.all_gather(tokens, 'tensor', axis=0, tiled=True)  36.8 us
    all_gather x1, waiting for transfers between devices, shards(): merged = lax.all_gather(merged_mine, 'tensor', axis=0, tiled=True)  32.5 us
    all_to_all x1, blocking collectives, shards(): lax.all_to_all(context, 'tensor', split_axis=0, concat_axis=0, tiled=True)  16 us
    sub x2, matrix products, attend(): exponent = jnp.exp(scores - row_max)  9.62 us
    all_gather x1, waiting for transfers between devices, shards(): w_out_all = lax.all_gather(w_out, 'tensor', axis=0, tiled=True)  8.44 us
  transfers between devices with their start and end apart: 4, of which 4 were waited for; matrix products, arithmetic and copies ran while one was open for 8% of the time, Pallas kernels for 0%

commit v1 on v0

--- a/solution.py
+++ b/solution.py
@@ -59,7 +59,9 @@
     tp_count = lax.axis_size("tensor")
     w_proj_all = lax.all_gather(w_proj, "dp", axis=0, tiled=True)
     w_out_all = lax.all_gather(w_out, "tensor", axis=0, tiled=True)
-    gathered = lax.all_gather(tokens, "tensor", axis=0, tiled=True)
+    gathered = jnp.concatenate(
+        lax.all_to_all(jnp.stack([tokens] * lax.axis_size("tensor")), "tensor", 0, 0), axis=0
+    )
     row_count = gathered.shape[0]
     local_rows = tokens.shape[0]
     normed = layer_norm(gathered, ln1_gain, ln1_shift).astype(jnp.bfloat16)

time: 340 us -> 315 us (0.926)
  waiting for transfers between devices: 226 us -> 197 us
  blocking collectives: 63.7 us -> 58.7 us
  other arithmetic: 5.21 us -> 9.83 us
  starting transfers between devices: 0.12 us -> 4.5 us
    all_to_all x0 -> x1, waiting for transfers between devices: none -> 50 us  [shards(): lax.all_to_all(jnp.stack([tokens] * lax.axis_size('tensor')), 'tensor', 0...]
    all_gather x1 -> x0, waiting for transfers between devices: 36.8 us -> none  [shards(): gathered = lax.all_gather(tokens, 'tensor', axis=0, tiled=True)]
    all_gather x1, waiting for transfers between devices: 147 us -> 113 us  [shards(): w_proj_all = lax.all_gather(w_proj, 'dp', axis=0, tiled=True)]
    all_gather x1, waiting for transfers between devices: 8.44 us -> 0.01 us  [shards(): w_out_all = lax.all_gather(w_out, 'tensor', axis=0, tiled=True)]
    all_to_all x1, blocking collectives: 16 us -> 11 us  [shards(): lax.all_to_all(context, 'tensor', split_axis=0, concat_axis=0, tiled=True)]
    all_to_all x0 -> x1, starting transfers between devices: none -> 4.42 us  [shards(): lax.all_to_all(jnp.stack([tokens] * lax.axis_size('tensor')), 'tensor', 0...]
  transfers between devices with their start and end apart: 4 -> 4, of which waited for: 4 -> 3; matrix products, arithmetic and copies ran while one was open for 8% -> 11% of each run, Pallas kernels for 0% -> 0%
where the time goes in v1:
time: 315 us
  waiting for transfers between devices  197 us (63%)
  blocking collectives  58.7 us (19%)
  matrix products  25.6 us (8%)
  between operations  13.3 us (4%)
  other arithmetic  9.83 us (3%)
  local copies, waits for them, and re-layouts  6.21 us (2%)
  starting transfers between devices  4.5 us (1%)
    all_gather x1, waiting for transfers between devices, shards(): w_proj_all = lax.all_gather(w_proj, 'dp', axis=0, tiled=True)  113 us
    all_to_all x1, waiting for transfers between devices, shards(): lax.all_to_all(jnp.stack([tokens] * lax.axis_size('tensor')), 'tensor', 0...  50 us
    all_to_all x1, blocking collectives, shards(): lax.all_to_all(outgoing, 'dp', split_axis=0, concat_axis=0, tiled=True)  47.7 us
    all_gather x1, waiting for transfers between devices, shards(): merged = lax.all_gather(merged_mine, 'tensor', axis=0, tiled=True)  32.6 us
    all_to_all x1, blocking collectives, shards(): lax.all_to_all(context, 'tensor', split_axis=0, concat_axis=0, tiled=True)  11 us
    sub x2, matrix products, attend(): exponent = jnp.exp(scores - row_max)  9.62 us
  transfers between devices with their start and end apart: 4, of which 3 were waited for; matrix products, arithmetic and copies ran while one was open for 11% of the time, Pallas kernels for 0%

profile of v1, /device:TPU:8, one launch (start us, length us, event | category | flops | bytes accessed | tf_op | source)
XLA Modules:
  0.0 314.8 jit_solution(6597091328763344059)
XLA Ops:
  6.5 0.0 copy-start
  6.5 0.0 all-gather.4.cloned.1.call-start
  6.5 0.7 all-gather.4.cloned.1.call-update
  7.3 0.0 all-gather.8.cloned.1.call-start
  7.3 0.7 all-gather.8.cloned.1.call-update
  8.0 0.0 copy-start.7
  8.0 2.9 stack.2
  10.9 4.4 %all-to-all-start = ((bf16[8,128,1408]{2,1,0:T(8,128)(2,1)}), bf16[8,128,1408]{2,1,0:T(8,128)(2,1)}, u32[]{:S(2)}, u32[]{:S(2)}) async-start(bf16[8,128,1408]{2,1,0:T(8,128)(2,1)} %stack.2), calls=%async_computation | async-start | bytes 5767168 | tf_op jit(solution)/shard_map/all_to_all | solution.py:63
  15.3 0.0 copy-start.3
  15.3 0.0 copy-start.4
  15.3 0.0 all-gather.6.cloned.1.call-start
  15.4 0.0 copy-done.7
  15.4 0.1 broadcast_in_dim.24
  15.5 0.1 eq.84
  15.6 0.1 broadcast_in_dim.28
  15.7 0.1 eq.89
  15.8 0.1 broadcast_in_dim.25
  15.9 0.1 eq.86
  16.0 0.7 broadcast_compare_fusion.1
  16.7 50.0 %all-to-all-done = bf16[8,128,1408]{2,1,0:T(8,128)(2,1)} async-done(((bf16[8,128,1408]{2,1,0:T(8,128)(2,1)}), bf16[8,128,1408]{2,1,0:T(8,128)(2,1)}, u32[]{:S(2)}, u32[]{:S(2)}) %all-to-all-start) | async-done | bytes 2883616 | tf_op jit(solution)/shard_map/all_to_all | solution.py:63
  66.7 2.3 convert_reduce_fusion
  69.0 2.7 fusion.4
  71.7 0.0 copy-done.3
  71.7 0.0 copy-done.4
  71.8 2.9 fusion.7
  74.7 0.0 copy-done
  74.7 2.9 convolution_convert_fusion
  77.6 4.8 %fusion.73 = (f32[2,512]{1,0:T(2,128)S(1)}, f32[2,512,1024]{2,1,0:T(8,128)}) fusion(pred[512,1024]{1,0:T(8,128)(4,1)S(1)} %get-tuple-element.5, bf16[1024,2,264]{0,2,1:T(8,128)(2,1)} %bitcast.66), kind=kOutput, calls=%fused_computation.81 | convolution fusion | flops 188744704 | bytes 5263360 | tf_op jit(solution)/shard_map/sub | solution.py:38
  82.4 0.0 copy-start.9
  82.4 4.8 %fusion.64 = (f32[2,512]{1,0:T(2,128)S(1)}, f32[2,512,1024]{2,1,0:T(8,128)}) fusion(pred[512,1024]{1,0:T(8,128)(4,1)S(1)} %get-tuple-element.6, bf16[1024,2,264]{0,2,1:T(8,128)(2,1)} %bitcast.67), kind=kOutput, calls=%fused_computation.80 | convolution fusion | flops 188744704 | bytes 5263360 | tf_op jit(solution)/shard_map/sub | solution.py:38
  87.2 0.0 copy-done.9
  87.2 0.0 copy-start.10
  87.2 3.2 %fusion.24 = bf16[512,2,88]{0,2,1:T(8,128)(2,1)S(1)} fusion(f32[2,512,1024]{2,1,0:T(8,128)} %get-tuple-element.12, f32[2,512]{1,0:T(2,128)S(1)} %get-tuple-element.11, bf16[1024,2,264]{0,2,1:T(8,128)(2,1)S(1)} %bitcast.68), kind=kOutput, calls=%fused_computation.36 | convolution fusion | flops 186736640 | bytes 4739072 | tf_op jit(solution)/shard_map/hqk,khd->qhd/dot_general | solution.py:40
  90.5 0.2 copy-done.10
  90.7 0.0 copy-start.1
  90.7 0.9 fusion.25
  91.6 0.0 copy-start.5
  91.6 0.0 copy-start.6
  91.7 0.1 copy.26
  91.8 11.0 %all_to_all.15 = bf16[8,128,176]{1,2,0:T(8,128)(2,1)S(1)} all-to-all(bf16[8,128,176]{1,2,0:T(8,128)(2,1)S(1)} %copy.22), channel_id=1, replica_groups=mesh['dp'=64,'tensor'=8] {'tensor'}, dimensions={0} | all-to-all | bytes 720896 | tf_op jit(solution)/shard_map/all_to_all | solution.py:75
  102.8 0.0 copy-start.2
  102.8 0.0 all-gather.4.cloned.1.call-done
  102.8 0.0 copy-done.1
  102.8 0.0 copy-start.8
  102.8 3.0 fusion.82
  105.8 0.2 multiply_reduce_fusion
  106.0 0.0 copy-done.5
  106.0 0.0 copy-done.6
  106.1 0.2 add_convert_fusion
  106.3 1.0 reshape.190
  107.2 0.0 all-gather.6.cloned.1.call-update
  107.3 0.0 copy-done.2
  107.3 0.6 reduce-window.6
  107.9 0.2 slice_reduce_fusion
  108.1 0.1 fusion.58
  108.2 112.5 %all-gather.8.cloned.1.call-done = bf16[5632,448]{1,0:T(8,128)(2,1)} async-done(((bf16[88,448]{1,0:T(8,128)(2,1)}), bf16[5632,448]{1,0:T(8,128)(2,1)}) %all-gather.8.cloned.1.call-update) | async-done | bytes 5046288 | tf_op jit(solution)/shard_map/all_gather | solution.py:60
  220.8 32.6 %all-gather.6.cloned.1.call-done = bf16[256,5632]{1,0:T(8,128)(2,1)} async-done(((bf16[32,5632]{1,0:T(8,128)(2,1)}), bf16[256,5632]{1,0:T(8,128)(2,1)}) %all-gather.6.cloned.1.call-update) | async-done | bytes 2883600 | tf_op jit(solution)/shard_map/all_gather | solution.py:81
  253.4 0.0 copy-done.8
  253.4 6.0 %convolution_convert_fusion.1 = bf16[512,448]{0,1:T(8,128)(2,1)S(1)} fusion(bf16[256,5632]{1,0:T(8,128)(2,1)} %all-gather.6.cloned.1.call-done, bf16[5632,448]{1,0:T(8,128)(2,1)} %all-gather.8.cloned.1.call-done, s32[256]{0:T(256)S(1)} %multiply_add_fusion, f32[448]{0:T(512)S(1)} %copy-done.8), kind=kOutput, calls=%fused_computation.31 | convolution fusion | flops 1409875968 | bytes 8391424 | tf_op jit(solution)/shard_map/dot_general | solution.py:94
  259.4 0.2 copy.23
  259.6 47.7 %all_to_all.16 = bf16[64,8,448]{2,1,0:T(8,128)(2,1)S(1)} all-to-all(bf16[64,8,448]{2,1,0:T(8,128)(2,1)S(1)} %bitcast.58), channel_id=1, replica_groups=mesh['dp'=64,'tensor'=8] {'dp'}, dimensions={0} | all-to-all | bytes 917504 | tf_op jit(solution)/shard_map/all_to_all | solution.py:98
  307.3 1.0 copy.24
  (11 shorter events, 0.2 us)
Async XLA Ops:
  6.5 68.2 %copy-start = (bf16[1408,2,264]{0,2,1:T(8,128)(2,1)S(1)}, bf16[1408,2,264]{0,2,1:T(8,128)(2,1)}, u32[]{:S(2)}) copy-start(bf16[1408,2,264]{0,2,1:T(8,128)(2,1)} %param.14) | copy-start | bytes 4460548
  6.5 96.2 %all-gather.4.cloned.1.call-start = ((), (), s32[]{:S(2)}) async-start(), calls=%async_computation.3 | async-start | bytes 4460544 | tf_op jit(solution)/shard_map/all_gather | solution.py:61
  7.3 213.5 %all-gather.8.cloned.1.call-start = ((), (), s32[]{:S(2)}) async-start(), calls=%async_computation.5 | async-start | bytes 5857280 | tf_op jit(solution)/shard_map/all_gather | solution.py:60
  8.0 7.4 %copy-start.7 = (s32[1,256]{1,0:T(1,128)S(1)}, s32[1,256]{1,0:T(1,128)}, u32[]{:S(2)}) copy-start(s32[1,256]{1,0:T(1,128)} %param.20) | copy-start | bytes 3076
  10.9 55.8 %all-to-all-start = ((bf16[8,128,1408]{2,1,0:T(8,128)(2,1)}), bf16[8,128,1408]{2,1,0:T(8,128)(2,1)}, u32[]{:S(2)}, u32[]{:S(2)}) async-start(bf16[8,128,1408]{2,1,0:T(8,128)(2,1)} %stack.2), calls=%async_computation | async-start | bytes 5767168 | tf_op jit(solution)/shard_map/all_to_all | solution.py:63
  15.3 56.4 %copy-start.3 = (f32[1408]{0:T(1024)S(1)}, f32[1408]{0:T(1024)}, u32[]{:S(2)}) copy-start(f32[1408]{0:T(1024)} %param.13) | copy-start | bytes 16900
  15.3 56.4 %copy-start.4 = (f32[1408]{0:T(1024)S(1)}, f32[1408]{0:T(1024)}, u32[]{:S(2)}) copy-start(f32[1408]{0:T(1024)} %param.12) | copy-start | bytes 16900
  15.3 238.1 %all-gather.6.cloned.1.call-start = ((), (), s32[]{:S(2)}) async-start(), calls=%async_computation.4 | async-start | bytes 3244032 | tf_op jit(solution)/shard_map/all_gather | solution.py:81
  82.4 4.8 %copy-start.9 = (bf16[1024,528]{0,1:T(8,128)(2,1)S(1)}, bf16[1024,528]{0,1:T(8,128)(2,1)}, u32[]{:S(2)}) copy-start(bf16[1024,528]{0,1:T(8,128)(2,1)} %convolution_convert_fusion) | copy-start | bytes 3244036
  87.2 3.5 %copy-start.10 = (f32[2,512,1024]{2,1,0:T(8,128)S(1)}, f32[2,512,1024]{2,1,0:T(8,128)}, u32[]{:S(2)}) copy-start(f32[2,512,1024]{2,1,0:T(8,128)} %get-tuple-element.10) | copy-start | bytes 12582916
  90.7 12.0 %copy-start.1 = (bf16[128,1408]{1,0:T(8,128)(2,1)S(1)}, bf16[128,1408]{1,0:T(8,128)(2,1)}, u32[]{:S(2)}) copy-start(bf16[128,1408]{1,0:T(8,128)(2,1)} %param.11) | copy-start | bytes 1081348
  91.6 14.4 %copy-start.5 = (f32[1408]{0:T(1024)S(1)}, f32[1408]{0:T(1024)}, u32[]{:S(2)}) copy-start(f32[1408]{0:T(1024)} %param.17) | copy-start | bytes 16900
  91.6 14.4 %copy-start.6 = (f32[1408]{0:T(1024)S(1)}, f32[1408]{0:T(1024)}, u32[]{:S(2)}) copy-start(f32[1408]{0:T(1024)} %param.16) | copy-start | bytes 16900
  102.8 4.5 %copy-start.2 = (s32[256,1]{0,1:T(1,128)S(1)}, s32[256,1]{0,1:T(1,128)}, u32[]{:S(2)}) copy-start(s32[256,1]{0,1:T(1,128)} %param.21) | copy-start | bytes 3076
  102.8 150.6 %copy-start.8 = (f32[448]{0:T(512)S(1)}, f32[448]{0:T(512)}, u32[]{:S(2)}) copy-start(f32[448]{0:T(512)} %param.19) | copy-start | bytes 5380
Sparse Core Ops, SparseCore 0:
  9.5 58.5 all-gather.3
  71.0 149.6 all-gather.7
  222.9 30.4 all-gather.5
